TPU v7x, 32 devices: a whole 2x2x4 slice. The times are simulated.
32 devices in a mesh: gz: 4 (over z), xy: 8 (over y, x, core).
Axes of the slice: x: 2, y: 2, z: 4, core: 2. Of those that a mesh axis runs over, the one named last changes fastest.
Arguments:
- tile_image: bfloat16 [4, 8, 4, 4, 2, 128], P('gz', 'xy'), may hold values from -6 to 6
- tile_target: bfloat16 [4, 8, 4, 3, 4, 2, 128], P('gz', 'xy'), may hold values from 0 to 1
- owner_counts: int32 [4, 8], P('gz', 'xy'), may hold values from 0 to 4, as said below
- tile_list: int32 [4, 8, 4], P('gz', 'xy'), may hold values from -1 to 15, as said below
- w_in: bfloat16 [27, 32], replicated, may hold values from -1.25 to 1.25
- w_res: bfloat16 [27, 32, 32], replicated, may hold values from -0.21875 to 0.21875
- w_down: bfloat16 [8, 64, 32], replicated, may hold values from -0.375 to 0.375
- w_mid: bfloat16 [27, 64, 64], replicated, may hold values from -0.15625 to 0.15625
- w_up: bfloat16 [8, 32, 64], replicated, may hold values from -0.75 to 0.75
- head_weight: bfloat16 [3, 32], replicated, may hold values from -1 to 1
Outputs:
- err_tiles: bfloat16 [4, 8, 4, 3, 4, 2, 128], P('gz', 'xy')
- grad_in: float32 [27, 32], replicated
- grad_res: float32 [27, 32, 32], replicated
- grad_down: float32 [8, 64, 32], replicated
- grad_mid: float32 [27, 64, 64], replicated
- grad_up: float32 [8, 32, 64], replicated
- head_weight_gradient: float32 [3, 32], replicated
Inputs may be any that keep to these rules, and one draw needn't show every extreme that they name: `owner_counts`: in each depth row the counts add up to 16, and some owner of every row holds exactly 4 tiles. `tile_list`: in each depth row the live slots (s < owner_counts) name every position 0 to 15 exactly once; the other slots hold -1.
All inputs are finite; a program needn't handle non-finite values.
Results may differ from a plain program's by a relative error of at most 0.0046.
Values may be sent and summed in bfloat16 or wider, within the bound.
No kernel may reach another device: no remote copies, remote signals or barrier semaphores. Data moves between devices by JAX's collectives and lax.ppermute only.
A program may use at most 64 MiB of HBM per device.

v0:
```python
import jax
import jax.numpy as jnp
from jax import lax
from jax.sharding import PartitionSpec as P

TPD = 2


def with_halo(cells, sides, width):
    for axis, dim in sides:
        count = lax.axis_size(axis)
        ends = count - 1
        head = lax.slice_in_dim(cells, 0, width, axis=dim)
        tail = lax.slice_in_dim(cells, cells.shape[dim] - width, cells.shape[dim], axis=dim)
        cells = jnp.concatenate(
            [
                lax.ppermute(tail, axis, [(i, (i + 1) % count) for i in range(ends)]),
                cells,
                lax.ppermute(head, axis, [((i + 1) % count, i) for i in range(ends)]),
            ],
            axis=dim,
        )
    return cells


def framed(field):
    padded = with_halo(field, (("gz", 1), ("xy", 3)), 1)
    return jnp.pad(padded, ((0, 0), (0, 0), (1, 1), (0, 0)))


def convolve(padded, weights):
    depth = padded.shape[1] - 2
    height = padded.shape[2] - 2
    width = padded.shape[3] - 2
    total = None
    for tap in range(27):
        off_z, off_y, off_x = (tap // 9, tap // 3 % 3, tap % 3)
        window = padded[:, off_z : off_z + depth, off_y : off_y + height, off_x : off_x + width]
        term = jnp.einsum("oc,czyx->ozyx", weights[tap], window, preferred_element_type=jnp.float32)
        total = term if total is None else total + term
    return total


def tap_grads(grad, padded):
    depth, height, width = grad.shape[1:]
    terms = []
    for tap in range(27):
        off_z, off_y, off_x = (tap // 9, tap // 3 % 3, tap % 3)
        window = padded[:, off_z : off_z + depth, off_y : off_y + height, off_x : off_x + width]
        terms.append(jnp.einsum("ozyx,czyx->oc", grad, window, preferred_element_type=jnp.float32))
    return jnp.stack(terms)


def flipped(weights):
    return jnp.transpose(weights[::-1], (0, 2, 1))


def strided(field, tap):
    return field[:, tap // 4 :: 2, tap // 2 % 2 :: 2, tap % 2 :: 2]


def alternate(parts):
    chans, depth, height, width = parts.shape[1:]
    return (
        parts.reshape(2, 2, 2, chans, depth, height, width)
        .transpose(3, 4, 0, 5, 1, 6, 2)
        .reshape(chans, 2 * depth, 2 * height, 2 * width)
    )


def local(
    tile_image, tile_target, owner_counts, tile_list, w_in, w_res, w_down, w_mid, w_up, head_weight
):
    single_float = jnp.float32
    brain_float_half = jnp.bfloat16
    ranks = lax.axis_size("xy")
    layers = lax.axis_size("gz")
    column = lax.axis_index("xy")
    slots = tile_list.shape[2]
    depth, height, width = (tile_image.shape[3], tile_image.shape[4], tile_image.shape[5])
    per_dev = TPD
    total_tiles = ranks * per_dev
    slot_list = tile_list[0, 0]
    live = jnp.arange(slots) < owner_counts[0, 0]
    select = ((slot_list[None, :] == jnp.arange(total_tiles)[:, None]) & live[None, :]).astype(
        brain_float_half
    )
    wanted = column * per_dev + jnp.arange(per_dev)
    piece_img = lax.all_gather(tile_image, "xy", axis=1, tiled=True)
    piece_tgt = lax.all_gather(tile_target, "xy", axis=1, tiled=True)
    piece_cnt = lax.all_gather(owner_counts, "xy", axis=1, tiled=True)
    piece_list = lax.all_gather(tile_list, "xy", axis=1, tiled=True)
    owners = piece_list.shape[1]
    piece_live = jnp.arange(slots)[None, :] < piece_cnt[0][:, None]
    match = ((piece_list[0][:, :, None] == wanted[None, None, :]) & piece_live[:, :, None]).astype(
        brain_float_half
    )
    acc_img = jnp.einsum(
        "kst,kszyx->tzyx", match, piece_img[0], preferred_element_type=single_float
    )
    acc_tgt = jnp.einsum(
        "kst,ksazyx->tazyx", match, piece_tgt[0], preferred_element_type=single_float
    )
    rows_hit = (jnp.arange(ranks)[:, None] == jnp.arange(owners)[None, :]).astype(single_float)
    acc_hit = jnp.dot(rows_hit, jnp.sum(match.astype(single_float), axis=1))
    acc_img, acc_tgt, acc_hit = (acc_img, acc_tgt, acc_hit)
    mine_img = acc_img.astype(brain_float_half)
    mine_tgt = acc_tgt.astype(brain_float_half)
    owner_hit = acc_hit.astype(brain_float_half)
    image = mine_img.transpose(1, 2, 0, 3).reshape(1, depth, height, per_dev * width)
    target = mine_tgt.transpose(1, 2, 3, 0, 4).reshape(3, depth, height, per_dev * width)
    voxel_cells = depth * height * per_dev * width * ranks * layers
    image_pad = framed(image)
    h0 = jax.nn.relu(convolve(image_pad, w_in[:, :, None])).astype(brain_float_half)
    h0_pad = framed(h0)
    h1 = jax.nn.relu(h0.astype(single_float) + convolve(h0_pad, w_res)).astype(brain_float_half)
    down_sum = None
    for tap in range(8):
        term = jnp.einsum(
            "oc,czyx->ozyx", w_down[tap], strided(h1, tap), preferred_element_type=single_float
        )
        down_sum = term if down_sum is None else down_sum + term
    dfield = jax.nn.relu(down_sum).astype(brain_float_half)
    dfield_pad = framed(dfield)
    cfield = jax.nn.relu(dfield.astype(single_float) + convolve(dfield_pad, w_mid)).astype(
        brain_float_half
    )
    upward = alternate(
        jnp.stack(
            [
                jnp.einsum("oc,czyx->ozyx", w_up[tap], cfield, preferred_element_type=single_float)
                for tap in range(8)
            ]
        )
    )
    signal_field = jax.nn.relu(h1.astype(single_float) + upward).astype(brain_float_half)
    logits = jnp.einsum(
        "ac,czyx->azyx", head_weight, signal_field, preferred_element_type=single_float
    )
    affinity_map = jax.nn.sigmoid(logits)
    error_field = affinity_map - target.astype(single_float)
    err_out = error_field.astype(brain_float_half)
    err_local = err_out.reshape(3, depth, height, per_dev, width).transpose(3, 0, 1, 2, 4)
    sending = owner_hit[:, :, None, None, None, None] * err_local[None]
    returned = lax.all_to_all(sending, "xy", split_axis=0, concat_axis=0, tiled=True)
    returned = returned.reshape((total_tiles, 3, depth, height, width))
    err_tiles = jnp.einsum(
        "ps,pazyx->sazyx", select, returned, preferred_element_type=single_float
    ).astype(brain_float_half)[None, None]
    logit_gradient = (error_field * affinity_map * (1.0 - affinity_map) / voxel_cells).astype(
        brain_float_half
    )
    head_weight_gradient = jnp.einsum(
        "mtnq,btnq->mb", logit_gradient, signal_field, preferred_element_type=single_float
    )
    gradient_total = jnp.einsum(
        "jn,jbrq->nbrq", head_weight, logit_gradient, preferred_element_type=single_float
    )
    gsf = jnp.where(signal_field > 0, gradient_total, 0.0).astype(brain_float_half)
    grad_up = jnp.stack(
        [
            jnp.einsum(
                "ozyx,czyx->oc", strided(gsf, tap), cfield, preferred_element_type=single_float
            )
            for tap in range(8)
        ]
    )
    gcoarse = None
    for tap in range(8):
        term = jnp.einsum(
            "oc,ozyx->czyx", w_up[tap], strided(gsf, tap), preferred_element_type=single_float
        )
        gcoarse = term if gcoarse is None else gcoarse + term
    gquad = jnp.where(cfield > 0, gcoarse, 0.0).astype(brain_float_half)
    grad_mid = tap_grads(gquad, dfield_pad)
    gdown = gquad.astype(single_float) + convolve(framed(gquad), flipped(w_mid))
    gdd = jnp.where(dfield > 0, gdown, 0.0).astype(brain_float_half)
    grad_down = jnp.stack(
        [
            jnp.einsum("ozyx,czyx->oc", gdd, strided(h1, tap), preferred_element_type=single_float)
            for tap in range(8)
        ]
    )
    spread = alternate(
        jnp.stack(
            [
                jnp.einsum("oc,ozyx->czyx", w_down[tap], gdd, preferred_element_type=single_float)
                for tap in range(8)
            ]
        )
    )
    gres = jnp.where(h1 > 0, gsf.astype(single_float) + spread, 0.0).astype(brain_float_half)
    grad_res = tap_grads(gres, h0_pad)
    gfirst = gres.astype(single_float) + convolve(framed(gres), flipped(w_res))
    gact = jnp.where(h0 > 0, gfirst, 0.0).astype(brain_float_half)
    grad_in = tap_grads(gact, image_pad)[:, :, 0]
    summed = lax.psum(
        (grad_in, grad_res, grad_down, grad_mid, grad_up, head_weight_gradient), ("gz", "xy")
    )
    return (err_tiles, summed[0], summed[1], summed[2], summed[3], summed[4], summed[5])


def solution(mesh):
    return jax.shard_map(
        local,
        mesh=mesh,
        in_specs=(
            P("gz", "xy", None, None, None, None),
            P("gz", "xy", None, None, None, None, None),
            P("gz", "xy"),
            P("gz", "xy", None),
            P(),
            P(),
            P(),
            P(),
            P(),
            P(),
        ),
        out_specs=(P("gz", "xy", None, None, None, None, None), P(), P(), P(), P(), P(), P()),
        check_vma=False,
    )
```

profile of v0, /device:TPU:0, one launch (start us, length us, event | category | flops | bytes accessed | tf_op | source)
XLA Modules:
  0.0 325.3 jit_solution(603947522372132895)
XLA Ops:
  9.8 9.5 %all-reduce.3 = s32[8]{0:T(128)S(1)} all-reduce(s32[8]{0:T(128)S(1)} %bitcast_dynamic-update-slice_fusion), channel_id=1, replica_groups=mesh['gz'=4,'xy'=8] {'xy'}, use_global_device_ids=true, to_apply=%add.3 | all-reduce | flops 8 | bytes 64
  19.3 8.1 %all_gather.12 = s32[1,8,4]{2,0,1:T(1,128)S(1)} all-gather(s32[1,1,4]{2,0,1:T(1,128)} %bitcast.2102), channel_id=1, replica_groups=mesh['gz'=4,'xy'=8] {'xy'}, dimensions={1}, use_global_device_ids=true | all-gather | bytes 144 | tf_op jit(solution)/shard_map/all_gather | solution.py:92
  28.2 8.9 %all_gather.14 = bf16[1,8,4,4,2,128]{5,3,4,2,0,1:T(4,128)(2,1)S(1)} all-gather(bf16[1,1,4,4,2,128]{5,3,4,2,0,1:T(4,128)(2,1)S(1)} %copy.229), channel_id=1, replica_groups=mesh['gz'=4,'xy'=8] {'xy'}, dimensions={1}, use_global_device_ids=true | all-gather | bytes 73728 | tf_op jit(solution)/shard_map/all_gather | solution.py:89
  37.4 3.5 %collective-permute-start = (bf16[1,1,2,256]{3,2,1,0:T(2,128)(2,1)S(1)}, bf16[1,1,2,256]{3,2,1,0:T(2,128)(2,1)S(1)}, u32[]{:S(2)}, u32[]{:S(2)}) collective-permute-start(bf16[1,1,2,256]{3,2,1,0:T(2,128)(2,1)S(1)} %get-tuple-element.194), channel_id=1, source_target_pairs={{0,8},{8,16},{16,24},{1,9},{9,17},{17,25},{2,10},{10,18},{18,26},{... | collective-permute-start | bytes 3080 | tf_op jit(solution)/shard_map/ppermute | solution.py:17
  40.9 1.3 collective-permute-start.1
  50.6 8.6 %all_gather.15 = bf16[1,8,4,3,4,2,128]{6,4,5,3,2,0,1:T(4,128)(2,1)S(1)} all-gather(bf16[1,1,4,3,4,2,128]{6,4,5,3,2,0,1:T(4,128)(2,1)S(1)} %copy.234), channel_id=1, replica_groups=mesh['gz'=4,'xy'=8] {'xy'}, dimensions={1}, use_global_device_ids=true | all-gather | bytes 221184 | tf_op jit(solution)/shard_map/all_gather | solution.py:90
  63.3 2.2 collective-permute-start.2
  65.5 1.3 collective-permute-start.3
  66.8 2.2 collective-permute-done.3
  71.3 4.5 %collective-permute-start.4 = (bf16[32,1,2,256]{3,0,2,1:T(8,128)(2,1)S(1)}, bf16[32,1,2,256]{3,0,2,1:T(8,128)(2,1)S(1)}, u32[]{:S(2)}, u32[]{:S(2)}) collective-permute-start(bf16[32,1,2,256]{3,0,2,1:T(8,128)(2,1)S(1)} %get-tuple-element.91), channel_id=1, source_target_pairs={{0,8},{8,16},{16,24},{1,9},{9,17},{17,25},{2,10},{10,18},{18,26},{... | collective-permute-start | bytes 98312 | tf_op jit(solution)/shard_map/ppermute | solution.py:17
  75.9 1.3 collective-permute-start.5
  77.5 4.2 %collective-permute-done.5 = bf16[32,1,2,256]{3,0,2,1:T(8,128)(2,1)S(1)} collective-permute-done((bf16[32,1,2,256]{3,0,2,1:T(8,128)(2,1)S(1)}, bf16[32,1,2,256]{3,0,2,1:T(8,128)(2,1)S(1)}, u32[]{:S(2)}, u32[]{:S(2)}) %collective-permute-start.5) | collective-permute-done | bytes 32800 | tf_op jit(solution)/shard_map/ppermute | solution.py:19
  81.8 2.8 collective-permute-start.6
  84.7 1.3 collective-permute-start.7
  86.2 2.6 collective-permute-done.7
  100.7 1.9 fusion.751
  105.3 3.5 %collective-permute-start.8 = (bf16[64,1,1,128]{3,0,1,2:T(8,128)(2,1)S(1)}, bf16[64,1,1,128]{3,0,1,2:T(8,128)(2,1)S(1)}, u32[]{:S(2)}, u32[]{:S(2)}) collective-permute-start(bf16[64,1,1,128]{3,0,1,2:T(8,128)(2,1)S(1)} %get-tuple-element.101), channel_id=1, source_target_pairs={{0,8},{8,16},{16,24},{1,9},{9,17},{17,25},{2,10},{10,18},{18,26},{... | collective-permute-start | bytes 49160 | tf_op jit(solution)/shard_map/ppermute | solution.py:17
  110.2 4.2 %collective-permute-done.9 = bf16[64,1,1,128]{3,0,1,2:T(8,128)(2,1)S(1)} collective-permute-done((bf16[64,1,1,128]{3,0,1,2:T(8,128)(2,1)S(1)}, bf16[64,1,1,128]{3,0,1,2:T(8,128)(2,1)S(1)}, u32[]{:S(2)}, u32[]{:S(2)}) %collective-permute-start.9) | collective-permute-done | bytes 16416 | tf_op jit(solution)/shard_map/ppermute | solution.py:19
  114.6 3.7 %collective-permute-start.10 = (bf16[64,4,1,1]{3,0,1,2:T(8,128)(2,1)S(1)}, bf16[64,4,1,1]{3,0,1,2:T(8,128)(2,1)S(1)}, u32[]{:S(2)}, u32[]{:S(2)}) collective-permute-start(bf16[64,4,1,1]{3,0,1,2:T(8,128)(2,1)S(1)} %get-tuple-element.95), channel_id=1, source_target_pairs={{0,1},{1,2},{2,3},{3,4},{4,5},{5,6},{6,7},{8,9},{9,10},{10,11},{11... | collective-permute-start | bytes 1544 | tf_op jit(solution)/shard_map/ppermute | solution.py:17
  118.3 1.5 collective-permute-start.11
  119.9 2.4 collective-permute-done.11
  138.8 3.5 %collective-permute-start.12 = (bf16[64,1,1,128]{3,0,1,2:T(8,128)(2,1)S(1)}, bf16[64,1,1,128]{3,0,1,2:T(8,128)(2,1)S(1)}, u32[]{:S(2)}, u32[]{:S(2)}) collective-permute-start(bf16[64,1,1,128]{3,0,1,2:T(8,128)(2,1)S(1)} %get-tuple-element.99), channel_id=1, source_target_pairs={{0,8},{8,16},{16,24},{1,9},{9,17},{17,25},{2,10},{10,18},{18,26},{... | collective-permute-start | bytes 49160 | tf_op jit(solution)/shard_map/ppermute | solution.py:17
  144.4 7.7 %all-to-all-start = ((bf16[8,2,3,4,2,128]{5,1,4,3,2,0:T(2,128)(2,1)}), bf16[8,2,3,4,2,128]{5,1,4,3,2,0:T(2,128)(2,1)S(1)}, u32[]{:S(2)}, u32[]{:S(2)}) async-start(bf16[8,2,3,4,2,128]{5,1,4,3,2,0:T(2,128)(2,1)} %broadcast_multiply_fusion), calls=%async_computation | async-start | bytes 196608 | tf_op jit(solution)/shard_map/all_to_all | solution.py:145
  153.6 3.0 collective-permute-start.14
  167.8 4.3 %collective-permute-start.16 = (bf16[32,1,2,256]{3,0,2,1:T(8,128)(2,1)S(1)}, bf16[32,1,2,256]{3,0,2,1:T(8,128)(2,1)S(1)}, u32[]{:S(2)}, u32[]{:S(2)}) collective-permute-start(bf16[32,1,2,256]{3,0,2,1:T(8,128)(2,1)S(1)} %get-tuple-element.81), channel_id=1, source_target_pairs={{0,8},{8,16},{16,24},{1,9},{9,17},{17,25},{2,10},{10,18},{18,26},{... | collective-permute-start | bytes 98312 | tf_op jit(solution)/shard_map/ppermute | solution.py:17
  175.1 2.8 collective-permute-done.17
  178.0 2.6 collective-permute-start.18
  182.1 5.0 %collective-permute-done.19 = bf16[32,6,2,1]{3,0,2,1:T(8,128)(2,1)S(1)} collective-permute-done((bf16[32,6,2,1]{3,0,2,1:T(8,128)(2,1)S(1)}, bf16[32,6,2,1]{3,0,2,1:T(8,128)(2,1)S(1)}, u32[]{:S(2)}, u32[]{:S(2)}) %collective-permute-start.19) | collective-permute-done | bytes 800 | tf_op jit(solution)/shard_map/ppermute | solution.py:19
  197.3 44.9 %all-reduce.4 = (f32[27,32]{1,0:T(8,128)}, f32[3,32]{1,0:T(4,128)}) all-reduce(f32[27,32]{1,0:T(8,128)S(1)} %bitcast.2093, f32[3,32]{1,0:T(4,128)S(1)} %copy-done.95), channel_id=1, replica_groups=mesh['gz'=4,'xy'=8] {'gz','xy'}, use_global_device_ids=true, to_apply=%region_1.2 | all-reduce | flops 960 | bytes 7680 | tf_op jit(solution)/shard_map/psum | solution.py:197
  243.1 70.2 %all-reduce.8.cloned.1.call-done = (f32[27,32,32]{2,1,0:T(8,128)}, f32[8,64,32]{1,2,0:T(8,128)}, f32[27,64,64]{2,1,0:T(8,128)}, f32[8,32,64]{2,1,0:T(8,128)}) async-done(((f32[27,32,32]{2,1,0:T(8,128)}, f32[8,64,32]{1,2,0:T(8,128)}, f32[27,64,64]{2,1,0:T(8,128)}, f32[8,32,64]{2,1,0:T(8,128)}), (f32[27,32,32]{2,1,0:T(8,128)}, f32[8,64,32]{1,2,0:T(8,128)}, f32[27,64,64]{2,1,0:T(8,128)}, ...) | async-done | bytes 684048 | tf_op jit(solution)/shard_map/psum | solution.py:197
  313.4 1.9 copy.810
  315.3 1.6 copy.811
  (544 shorter events, 81.4 us)
Async XLA Ops:
  7.2 119.9 %copy-start = (bf16[3,32]{1,0:T(4,128)(2,1)S(1)}, bf16[3,32]{1,0:T(4,128)(2,1)}, u32[]{:S(2)}) copy-start(bf16[3,32]{1,0:T(4,128)(2,1)} %param.19) | copy-start | bytes 580
  37.4 25.2 %collective-permute-start = (bf16[1,1,2,256]{3,2,1,0:T(2,128)(2,1)S(1)}, bf16[1,1,2,256]{3,2,1,0:T(2,128)(2,1)S(1)}, u32[]{:S(2)}, u32[]{:S(2)}) collective-permute-start(bf16[1,1,2,256]{3,2,1,0:T(2,128)(2,1)S(1)} %get-tuple-element.194), channel_id=1, source_target_pairs={{0,8},{8,16},{16,24},{1,9},{9,17},{17,25},{2,10},{10,18},{18,26},{... | collective-permute-start | bytes 3080 | tf_op jit(solution)/shard_map/ppermute | solution.py:17
  40.9 21.7 %collective-permute-start.1 = (bf16[1,1,2,256]{3,2,1,0:T(2,128)(2,1)S(1)}, bf16[1,1,2,256]{3,2,1,0:T(2,128)(2,1)S(1)}, u32[]{:S(2)}, u32[]{:S(2)}) collective-permute-start(bf16[1,1,2,256]{3,2,1,0:T(2,128)(2,1)S(1)} %get-tuple-element.193), channel_id=1, source_target_pairs={{8,0},{16,8},{24,16},{9,1},{17,9},{25,17},{10,2},{18,10},{26,18},{... | collective-permute-start | bytes 3080 | tf_op jit(solution)/shard_map/ppermute | solution.py:19
  48.0 12.4 %copy-start.4 = (bf16[27,32,32]{2,1,0:T(8,128)(2,1)S(1)}, bf16[27,32,32]{2,1,0:T(8,128)(2,1)}, u32[]{:S(2)}) copy-start(bf16[27,32,32]{2,1,0:T(8,128)(2,1)} %param.15) | copy-start | bytes 165892
  63.3 3.6 %collective-permute-start.2 = (bf16[1,6,2,1]{3,2,1,0:T(2,128)(2,1)S(1)}, bf16[1,6,2,1]{3,2,1,0:T(2,128)(2,1)S(1)}, u32[]{:S(2)}, u32[]{:S(2)}) collective-permute-start(bf16[1,6,2,1]{3,2,1,0:T(2,128)(2,1)S(1)} %get-tuple-element.184), channel_id=1, source_target_pairs={{0,1},{1,2},{2,3},{3,4},{4,5},{5,6},{6,7},{8,9},{9,10},{10,11},{11... | collective-permute-start | bytes 80 | tf_op jit(solution)/shard_map/ppermute | solution.py:17
  65.5 3.5 %collective-permute-start.3 = (bf16[1,6,2,1]{3,2,1,0:T(2,128)(2,1)S(1)}, bf16[1,6,2,1]{3,2,1,0:T(2,128)(2,1)S(1)}, u32[]{:S(2)}, u32[]{:S(2)}) collective-permute-start(bf16[1,6,2,1]{3,2,1,0:T(2,128)(2,1)S(1)} %get-tuple-element.185), channel_id=1, source_target_pairs={{1,0},{2,1},{3,2},{4,3},{5,4},{6,5},{7,6},{9,8},{10,9},{11,10},{12... | collective-permute-start | bytes 80 | tf_op jit(solution)/shard_map/ppermute | solution.py:19
  71.3 6.1 %collective-permute-start.4 = (bf16[32,1,2,256]{3,0,2,1:T(8,128)(2,1)S(1)}, bf16[32,1,2,256]{3,0,2,1:T(8,128)(2,1)S(1)}, u32[]{:S(2)}, u32[]{:S(2)}) collective-permute-start(bf16[32,1,2,256]{3,0,2,1:T(8,128)(2,1)S(1)} %get-tuple-element.91), channel_id=1, source_target_pairs={{0,8},{8,16},{16,24},{1,9},{9,17},{17,25},{2,10},{10,18},{18,26},{... | collective-permute-start | bytes 98312 | tf_op jit(solution)/shard_map/ppermute | solution.py:17
  75.9 5.8 %collective-permute-start.5 = (bf16[32,1,2,256]{3,0,2,1:T(8,128)(2,1)S(1)}, bf16[32,1,2,256]{3,0,2,1:T(8,128)(2,1)S(1)}, u32[]{:S(2)}, u32[]{:S(2)}) collective-permute-start(bf16[32,1,2,256]{3,0,2,1:T(8,128)(2,1)S(1)} %get-tuple-element.92), channel_id=1, source_target_pairs={{8,0},{16,8},{24,16},{9,1},{17,9},{25,17},{10,2},{18,10},{26,18},{... | collective-permute-start | bytes 98312 | tf_op jit(solution)/shard_map/ppermute | solution.py:19
  81.8 4.4 %collective-permute-start.6 = (bf16[32,6,2,1]{3,0,2,1:T(8,128)(2,1)S(1)}, bf16[32,6,2,1]{3,0,2,1:T(8,128)(2,1)S(1)}, u32[]{:S(2)}, u32[]{:S(2)}) collective-permute-start(bf16[32,6,2,1]{3,0,2,1:T(8,128)(2,1)S(1)} %get-tuple-element.79), channel_id=1, source_target_pairs={{0,1},{1,2},{2,3},{3,4},{4,5},{5,6},{6,7},{8,9},{9,10},{10,11},{11... | collective-permute-start | bytes 2312 | tf_op jit(solution)/shard_map/ppermute | solution.py:17
  84.7 4.2 %collective-permute-start.7 = (bf16[32,6,2,1]{3,0,2,1:T(8,128)(2,1)S(1)}, bf16[32,6,2,1]{3,0,2,1:T(8,128)(2,1)S(1)}, u32[]{:S(2)}, u32[]{:S(2)}) collective-permute-start(bf16[32,6,2,1]{3,0,2,1:T(8,128)(2,1)S(1)} %get-tuple-element.80), channel_id=1, source_target_pairs={{1,0},{2,1},{3,2},{4,3},{5,4},{6,5},{7,6},{9,8},{10,9},{11,10},{12... | collective-permute-start | bytes 2312 | tf_op jit(solution)/shard_map/ppermute | solution.py:19
  95.4 8.2 %copy-start.39 = (bf16[32,2,1,128]{3,0,2,1:T(8,128)(2,1)}, bf16[32,2,1,128]{3,0,2,1:T(8,128)(2,1)S(1)}, u32[]{:S(2)}) copy-start(bf16[32,2,1,128]{3,0,2,1:T(8,128)(2,1)S(1)} %slice.1254) | copy-start | bytes 49156
  104.2 18.4 %copy-start.20 = (f32[2,128,64]{1,2,0:T(8,128)S(1)}, f32[2,128,64]{1,2,0:T(8,128)}, u32[]{:S(2)}) copy-start(f32[2,128,64]{1,2,0:T(8,128)} %convolution_add_fusion.42) | copy-start | bytes 196612
  105.3 4.9 %collective-permute-start.8 = (bf16[64,1,1,128]{3,0,1,2:T(8,128)(2,1)S(1)}, bf16[64,1,1,128]{3,0,1,2:T(8,128)(2,1)S(1)}, u32[]{:S(2)}, u32[]{:S(2)}) collective-permute-start(bf16[64,1,1,128]{3,0,1,2:T(8,128)(2,1)S(1)} %get-tuple-element.101), channel_id=1, source_target_pairs={{0,8},{8,16},{16,24},{1,9},{9,17},{17,25},{2,10},{10,18},{18,26},{... | collective-permute-start | bytes 49160 | tf_op jit(solution)/shard_map/ppermute | solution.py:17
  108.8 5.6 %collective-permute-start.9 = (bf16[64,1,1,128]{3,0,1,2:T(8,128)(2,1)S(1)}, bf16[64,1,1,128]{3,0,1,2:T(8,128)(2,1)S(1)}, u32[]{:S(2)}, u32[]{:S(2)}) collective-permute-start(bf16[64,1,1,128]{3,0,1,2:T(8,128)(2,1)S(1)} %get-tuple-element.102), channel_id=1, source_target_pairs={{8,0},{16,8},{24,16},{9,1},{17,9},{25,17},{10,2},{18,10},{26,18},{... | collective-permute-start | bytes 49160 | tf_op jit(solution)/shard_map/ppermute | solution.py:19
  114.6 8.0 %collective-permute-start.10 = (bf16[64,4,1,1]{3,0,1,2:T(8,128)(2,1)S(1)}, bf16[64,4,1,1]{3,0,1,2:T(8,128)(2,1)S(1)}, u32[]{:S(2)}, u32[]{:S(2)}) collective-permute-start(bf16[64,4,1,1]{3,0,1,2:T(8,128)(2,1)S(1)} %get-tuple-element.95), channel_id=1, source_target_pairs={{0,1},{1,2},{2,3},{3,4},{4,5},{5,6},{6,7},{8,9},{9,10},{10,11},{11... | collective-permute-start | bytes 1544 | tf_op jit(solution)/shard_map/ppermute | solution.py:17
  118.3 4.0 %collective-permute-start.11 = (bf16[64,4,1,1]{3,0,1,2:T(8,128)(2,1)S(1)}, bf16[64,4,1,1]{3,0,1,2:T(8,128)(2,1)S(1)}, u32[]{:S(2)}, u32[]{:S(2)}) collective-permute-start(bf16[64,4,1,1]{3,0,1,2:T(8,128)(2,1)S(1)} %get-tuple-element.96), channel_id=1, source_target_pairs={{1,0},{2,1},{3,2},{4,3},{5,4},{6,5},{7,6},{9,8},{10,9},{11,10},{12... | collective-permute-start | bytes 1544 | tf_op jit(solution)/shard_map/ppermute | solution.py:19
  127.7 9.2 %copy-start.9 = (bf16[32,4,2,256]{3,0,2,1:T(8,128)(2,1)}, bf16[32,4,2,256]{3,0,2,1:T(8,128)(2,1)S(1)}, u32[]{:S(2)}) copy-start(bf16[32,4,2,256]{3,0,2,1:T(8,128)(2,1)S(1)} %fusion.40) | copy-start | bytes 393220
  138.2 19.3 %copy-start.21 = (f32[2,128,64]{1,2,0:T(8,128)S(1)}, f32[2,128,64]{1,2,0:T(8,128)}, u32[]{:S(2)}) copy-start(f32[2,128,64]{1,2,0:T(8,128)} %fusion.310) | copy-start | bytes 196612
  138.2 19.3 %copy-start.22 = (f32[2,128,64]{1,2,0:T(8,128)S(1)}, f32[2,128,64]{1,2,0:T(8,128)}, u32[]{:S(2)}) copy-start(f32[2,128,64]{1,2,0:T(8,128)} %convolution_add_fusion.31) | copy-start | bytes 196612
  138.8 13.4 %collective-permute-start.12 = (bf16[64,1,1,128]{3,0,1,2:T(8,128)(2,1)S(1)}, bf16[64,1,1,128]{3,0,1,2:T(8,128)(2,1)S(1)}, u32[]{:S(2)}, u32[]{:S(2)}) collective-permute-start(bf16[64,1,1,128]{3,0,1,2:T(8,128)(2,1)S(1)} %get-tuple-element.99), channel_id=1, source_target_pairs={{0,8},{8,16},{16,24},{1,9},{9,17},{17,25},{2,10},{10,18},{18,26},{... | collective-permute-start | bytes 49160 | tf_op jit(solution)/shard_map/ppermute | solution.py:17
  142.3 9.9 %collective-permute-start.13 = (bf16[64,1,1,128]{3,0,1,2:T(8,128)(2,1)S(1)}, bf16[64,1,1,128]{3,0,1,2:T(8,128)(2,1)S(1)}, u32[]{:S(2)}, u32[]{:S(2)}) collective-permute-start(bf16[64,1,1,128]{3,0,1,2:T(8,128)(2,1)S(1)} %get-tuple-element.100), channel_id=1, source_target_pairs={{8,0},{16,8},{24,16},{9,1},{17,9},{25,17},{10,2},{18,10},{26,18},{... | collective-permute-start | bytes 49160 | tf_op jit(solution)/shard_map/ppermute | solution.py:19
  144.4 14.0 %copy-start.2 = (f32[27,64,64]{2,1,0:T(8,128)}, f32[27,64,64]{2,1,0:T(8,128)S(1)}, u32[]{:S(2)}) copy-start(f32[27,64,64]{2,1,0:T(8,128)S(1)} %constant_dynamic-update-slice_fusion.3) | copy-start | bytes 1327108
  144.4 97.8 %all-to-all-start = ((bf16[8,2,3,4,2,128]{5,1,4,3,2,0:T(2,128)(2,1)}), bf16[8,2,3,4,2,128]{5,1,4,3,2,0:T(2,128)(2,1)S(1)}, u32[]{:S(2)}, u32[]{:S(2)}) async-start(bf16[8,2,3,4,2,128]{5,1,4,3,2,0:T(2,128)(2,1)} %broadcast_multiply_fusion), calls=%async_computation | async-start | bytes 196608 | tf_op jit(solution)/shard_map/all_to_all | solution.py:145
  152.1 161.2 %all-reduce.8.cloned.1.call-start = ((), (), s32[]{:S(2)}) async-start(), calls=%async_computation.1 | async-start | bytes 3178496 | tf_op jit(solution)/shard_map/psum | solution.py:197
  152.3 4.5 %collective-permute-start.15 = (bf16[64,4,1,1]{3,0,1,2:T(8,128)(2,1)S(1)}, bf16[64,4,1,1]{3,0,1,2:T(8,128)(2,1)S(1)}, u32[]{:S(2)}, u32[]{:S(2)}) collective-permute-start(bf16[64,4,1,1]{3,0,1,2:T(8,128)(2,1)S(1)} %get-tuple-element.94), channel_id=1, source_target_pairs={{1,0},{2,1},{3,2},{4,3},{5,4},{6,5},{7,6},{9,8},{10,9},{11,10},{12... | collective-permute-start | bytes 1544 | tf_op jit(solution)/shard_map/ppermute | solution.py:19
  153.6 3.9 %collective-permute-start.14 = (bf16[64,4,1,1]{3,0,1,2:T(8,128)(2,1)S(1)}, bf16[64,4,1,1]{3,0,1,2:T(8,128)(2,1)S(1)}, u32[]{:S(2)}, u32[]{:S(2)}) collective-permute-start(bf16[64,4,1,1]{3,0,1,2:T(8,128)(2,1)S(1)} %get-tuple-element.93), channel_id=1, source_target_pairs={{0,1},{1,2},{2,3},{3,4},{4,5},{5,6},{6,7},{8,9},{9,10},{10,11},{11... | collective-permute-start | bytes 1544 | tf_op jit(solution)/shard_map/ppermute | solution.py:17
  167.8 7.3 %collective-permute-start.16 = (bf16[32,1,2,256]{3,0,2,1:T(8,128)(2,1)S(1)}, bf16[32,1,2,256]{3,0,2,1:T(8,128)(2,1)S(1)}, u32[]{:S(2)}, u32[]{:S(2)}) collective-permute-start(bf16[32,1,2,256]{3,0,2,1:T(8,128)(2,1)S(1)} %get-tuple-element.81), channel_id=1, source_target_pairs={{0,8},{8,16},{16,24},{1,9},{9,17},{17,25},{2,10},{10,18},{18,26},{... | collective-permute-start | bytes 98312 | tf_op jit(solution)/shard_map/ppermute | solution.py:17
  172.1 5.8 %collective-permute-start.17 = (bf16[32,1,2,256]{3,0,2,1:T(8,128)(2,1)S(1)}, bf16[32,1,2,256]{3,0,2,1:T(8,128)(2,1)S(1)}, u32[]{:S(2)}, u32[]{:S(2)}) collective-permute-start(bf16[32,1,2,256]{3,0,2,1:T(8,128)(2,1)S(1)} %get-tuple-element.82), channel_id=1, source_target_pairs={{8,0},{16,8},{24,16},{9,1},{17,9},{25,17},{10,2},{18,10},{26,18},{... | collective-permute-start | bytes 98312 | tf_op jit(solution)/shard_map/ppermute | solution.py:19
  178.0 4.1 %collective-permute-start.18 = (bf16[32,6,2,1]{3,0,2,1:T(8,128)(2,1)S(1)}, bf16[32,6,2,1]{3,0,2,1:T(8,128)(2,1)S(1)}, u32[]{:S(2)}, u32[]{:S(2)}) collective-permute-start(bf16[32,6,2,1]{3,0,2,1:T(8,128)(2,1)S(1)} %get-tuple-element.75), channel_id=1, source_target_pairs={{0,1},{1,2},{2,3},{3,4},{4,5},{5,6},{6,7},{8,9},{9,10},{10,11},{11... | collective-permute-start | bytes 2312 | tf_op jit(solution)/shard_map/ppermute | solution.py:17
  180.7 6.5 %collective-permute-start.19 = (bf16[32,6,2,1]{3,0,2,1:T(8,128)(2,1)S(1)}, bf16[32,6,2,1]{3,0,2,1:T(8,128)(2,1)S(1)}, u32[]{:S(2)}, u32[]{:S(2)}) collective-permute-start(bf16[32,6,2,1]{3,0,2,1:T(8,128)(2,1)S(1)} %get-tuple-element.76), channel_id=1, source_target_pairs={{1,0},{2,1},{3,2},{4,3},{5,4},{6,5},{7,6},{9,8},{10,9},{11,10},{12... | collective-permute-start | bytes 2312 | tf_op jit(solution)/shard_map/ppermute | solution.py:19
  195.9 46.4 %copy-start.96 = (s32[1,1,4]{2,1,0:T(1,128)S(1)}, s32[1,1,4]{2,1,0:T(1,128)}, u32[]{:S(2)}) copy-start(s32[1,1,4]{2,1,0:T(1,128)} %param.13) | copy-start | bytes 52
  195.9 46.4 %copy-start.97 = (pred[4]{0:T(512)(128)(4,1)S(1)}, pred[4]{0:T(512)(128)(4,1)}, u32[]{:S(2)}) copy-start(pred[4]{0:T(512)(128)(4,1)} %iota_compare_fusion.8) | copy-start | bytes 16
  (88 other events, 208.0 us)
Sparse Core Ops, SparseCore 0:
  175.2 138.1 all-reduce.7
where the time goes:
time: 327 us; the launch traced here: 325 us
  waiting for transfers between devices  94.4 us (29%)
  blocking collectives  80 us (24%)
  starting transfers between devices  54.6 us (17%)
  matrix products  41.6 us (13%)
  local copies, waits for them, and re-layouts  30.6 us (9%)
  between operations  16.7 us (5%)
  other arithmetic  7.44 us (2%)
    psum x1, waiting for transfers between devices, local(): lax.psum((grad_in, grad_res, grad_down, grad_mid, grad_up, head_weight_gr...  70.2 us
    psum x1, blocking collectives, local(): lax.psum((grad_in, grad_res, grad_down, grad_mid, grad_up, head_weight_gr...  44.9 us
    ppermute x10, starting transfers between devices, with_halo(): lax.ppermute(tail, axis, [(i, (i + 1) % count) for i in range(ends)])  33.7 us
    ppermute x10, waiting for transfers between devices, with_halo(): lax.ppermute(head, axis, [((i + 1) % count, i) for i in range(ends)])  23.5 us
    dot_general x108, matrix products, convolve(): jnp.einsum('oc,czyx->ozyx', weights[tap], window, preferred_element_type=...  22.8 us
    ppermute x10, starting transfers between devices, with_halo(): lax.ppermute(head, axis, [((i + 1) % count, i) for i in range(ends)])  13.1 us
    unnamed x226, local copies, waits for them, and re-layouts  12 us
    slice x16, local copies, waits for them, and re-layouts, strided(): return field[:, tap // 4::2, tap // 2 % 2::2, tap % 2::2]  11.8 us
  transfers between devices with their start and end apart: 22, of which 10 were waited for; matrix products, arithmetic and copies ran while one was open for 11% of the time, Pallas kernels for 0%

commit v1 on v0

--- a/solution.py
+++ b/solution.py
@@ -2,6 +2,7 @@
 import jax.numpy as jnp
 from jax import lax
 from jax.sharding import PartitionSpec as P
+from jax.lax import axis_index, axis_size, ppermute
 
 TPD = 2
 
@@ -87,7 +88,30 @@
     )
     wanted = column * per_dev + jnp.arange(per_dev)
     piece_img = lax.all_gather(tile_image, "xy", axis=1, tiled=True)
-    piece_tgt = lax.all_gather(tile_target, "xy", axis=1, tiled=True)
+    s_next = axis_size("xy")
+    val2, back, aux = (s_next, axis_index("xy"), tile_target.shape[1])
+    line_up = []
+    for hop_no in tuple(range(val2)):
+        line_up.append((hop_no, (hop_no + 1) % val2))
+    so_far_all = []
+    for hop_no in tuple(range(val2)):
+        so_far_all.append((hop_no, (hop_no - 1) % val2))
+    piece_tgt = jnp.zeros(
+        (*tile_target.shape[:1], val2 * aux, *tile_target.shape[2:]), tile_target.dtype
+    )
+    piece_tgt = lax.dynamic_update_slice_in_dim(piece_tgt, tile_target, back * aux, axis=1)
+    low = piece_next = tile_target
+    high = val2 // 2
+    for kk in tuple(range(1, high + 1)):
+        low = ppermute(low, "xy", line_up)
+        piece_tgt = lax.dynamic_update_slice_in_dim(
+            piece_tgt, low, (back - kk) % val2 * aux, axis=1
+        )
+        if kk < val2 - high:
+            piece_next = ppermute(piece_next, "xy", so_far_all)
+            piece_tgt = lax.dynamic_update_slice_in_dim(
+                piece_tgt, piece_next, (back + kk) % val2 * aux, axis=1
+            )
     piece_cnt = lax.all_gather(owner_counts, "xy", axis=1, tiled=True)
     piece_list = lax.all_gather(tile_list, "xy", axis=1, tiled=True)
     owners = piece_list.shape[1]

time: 327 us -> 339 us (1.037)
  local copies, waits for them, and re-layouts: 30.6 us -> 46.3 us
  starting transfers between devices: 54.6 us -> 64.1 us
  blocking collectives: 80 us -> 71.3 us
  waiting for transfers between devices: 94.4 us -> 88.6 us
    dynamic_update_slice x0 -> x8, local copies, waits for them, and re-layouts: none -> 14.2 us  [the longest x4 7.12 us: local(): lax.dynamic_update_slice_in_dim(piece_tgt, low, (back - kk) % val2 * aux,...]
    ppermute x0 -> x7, starting transfers between devices: none -> 12.4 us  [the longest x4 8.89 us: local(): low = ppermute(low, 'xy', line_up)]
    all_gather x1 -> x0, blocking collectives: 8.6 us -> none  [local(): piece_tgt = lax.all_gather(tile_target, 'xy', axis=1, tiled=True)]
    ppermute x10, waiting for transfers between devices: 23.5 us -> 17.5 us  [with_halo(): lax.ppermute(head, axis, [((i + 1) % count, i) for i in range(ends)])]
    unnamed x226 -> x235, local copies, waits for them, and re-layouts: 12 us -> 12.3 us
  transfers between devices with their start and end apart: 22 -> 29, of which waited for: 10 -> 7; matrix products, arithmetic and copies ran while one was open for 11% -> 22% of each run, Pallas kernels for 0% -> 0%
where the time goes in v1:
time: 339 us; the launch traced here: 337 us
  waiting for transfers between devices  88.6 us (26%)
  blocking collectives  71.3 us (21%)
  starting transfers between devices  64.1 us (19%)
  local copies, waits for them, and re-layouts  46.3 us (14%)
  matrix products  42.8 us (13%)
  between operations  17 us (5%)
  other arithmetic  7.49 us (2%)
    psum x1, waiting for transfers between devices, local(): lax.psum((grad_in, grad_res, grad_down, grad_mid, grad_up, head_weight_gr...  70.5 us
    psum x1, blocking collectives, local(): lax.psum((grad_in, grad_res, grad_down, grad_mid, grad_up, head_weight_gr...  46.2 us
    ppermute x10, starting transfers between devices, with_halo(): lax.ppermute(tail, axis, [(i, (i + 1) % count) for i in range(ends)])  33.1 us
    dot_general x108, matrix products, convolve(): jnp.einsum('oc,czyx->ozyx', weights[tap], window, preferred_element_type=...  24 us
    ppermute x10, waiting for transfers between devices, with_halo(): lax.ppermute(head, axis, [((i + 1) % count, i) for i in range(ends)])  17.5 us
    ppermute x10, starting transfers between devices, with_halo(): lax.ppermute(head, axis, [((i + 1) % count, i) for i in range(ends)])  13.4 us
    unnamed x235, local copies, waits for them, and re-layouts  12.3 us
    slice x16, local copies, waits for them, and re-layouts, strided(): return field[:, tap // 4::2, tap // 2 % 2::2, tap % 2::2]  11.8 us
  transfers between devices with their start and end apart: 29, of which 7 were waited for; matrix products, arithmetic and copies ran while one was open for 22% of the time, Pallas kernels for 0%

profile of v1, /device:TPU:0, one launch (start us, length us, event | category | flops | bytes accessed | tf_op | source)
XLA Modules:
  0.0 337.5 jit_solution(1718762251031828880)
XLA Ops:
  7.7 2.9 collective-permute-start.13
  13.3 8.1 %all-reduce.3 = s32[8]{0:T(128)S(1)} all-reduce(s32[8]{0:T(128)S(1)} %bitcast_dynamic-update-slice_fusion), channel_id=1, replica_groups=mesh['gz'=4,'xy'=8] {'xy'}, use_global_device_ids=true, to_apply=%add.3 | all-reduce | flops 8 | bytes 64
  21.4 8.5 %all_gather.9 = s32[1,8,4]{2,0,1:T(1,128)S(1)} all-gather(s32[1,1,4]{2,0,1:T(1,128)} %bitcast.2114), channel_id=1, replica_groups=mesh['gz'=4,'xy'=8] {'xy'}, dimensions={1}, use_global_device_ids=true | all-gather | bytes 144 | tf_op jit(solution)/shard_map/all_gather | solution.py:116
  30.6 8.6 %all_gather.11 = bf16[1,8,4,4,2,128]{5,3,4,2,0,1:T(4,128)(2,1)S(1)} all-gather(bf16[1,1,4,4,2,128]{5,3,4,2,0,1:T(4,128)(2,1)S(1)} %copy.249), channel_id=1, replica_groups=mesh['gz'=4,'xy'=8] {'xy'}, dimensions={1}, use_global_device_ids=true | all-gather | bytes 73728 | tf_op jit(solution)/shard_map/all_gather | solution.py:90
  39.5 3.5 %collective-permute-start = (bf16[1,1,2,256]{3,2,1,0:T(2,128)(2,1)S(1)}, bf16[1,1,2,256]{3,2,1,0:T(2,128)(2,1)S(1)}, u32[]{:S(2)}, u32[]{:S(2)}) collective-permute-start(bf16[1,1,2,256]{3,2,1,0:T(2,128)(2,1)S(1)} %get-tuple-element.194), channel_id=1, source_target_pairs={{0,8},{8,16},{16,24},{1,9},{9,17},{17,25},{2,10},{10,18},{18,26},{... | collective-permute-start | bytes 3080 | tf_op jit(solution)/shard_map/ppermute | solution.py:18
  56.4 1.8 dynamic_update_slice.32
  59.0 2.0 collective-permute-start.2
  62.2 2.5 collective-permute-done.3
  67.1 4.5 %collective-permute-start.4 = (bf16[32,1,2,256]{3,0,2,1:T(8,128)(2,1)S(1)}, bf16[32,1,2,256]{3,0,2,1:T(8,128)(2,1)S(1)}, u32[]{:S(2)}, u32[]{:S(2)}) collective-permute-start(bf16[32,1,2,256]{3,0,2,1:T(8,128)(2,1)S(1)} %get-tuple-element.91), channel_id=1, source_target_pairs={{0,8},{8,16},{16,24},{1,9},{9,17},{17,25},{2,10},{10,18},{18,26},{... | collective-permute-start | bytes 98312 | tf_op jit(solution)/shard_map/ppermute | solution.py:18
  73.2 1.8 dynamic_update_slice.33
  75.0 1.8 dynamic_update_slice.34
  76.8 2.1 collective-permute-start.14
  79.6 1.8 collective-permute-start.6
  83.6 2.5 collective-permute-done.7
  97.9 1.9 fusion.749
  102.6 4.3 %collective-permute-start.8 = (bf16[64,1,1,128]{3,0,1,2:T(8,128)(2,1)S(1)}, bf16[64,1,1,128]{3,0,1,2:T(8,128)(2,1)S(1)}, u32[]{:S(2)}, u32[]{:S(2)}) collective-permute-start(bf16[64,1,1,128]{3,0,1,2:T(8,128)(2,1)S(1)} %get-tuple-element.101), channel_id=1, source_target_pairs={{0,8},{8,16},{16,24},{1,9},{9,17},{17,25},{2,10},{10,18},{18,26},{... | collective-permute-start | bytes 49160 | tf_op jit(solution)/shard_map/ppermute | solution.py:18
  109.9 1.8 dynamic_update_slice.35
  111.6 1.8 dynamic_update_slice.36
  113.4 3.0 collective-permute-start.16
  116.6 2.5 collective-permute-start.10
  120.6 4.9 %collective-permute-done.11 = bf16[64,4,1,1]{3,0,1,2:T(8,128)(2,1)S(1)} collective-permute-done((bf16[64,4,1,1]{3,0,1,2:T(8,128)(2,1)S(1)}, bf16[64,4,1,1]{3,0,1,2:T(8,128)(2,1)S(1)}, u32[]{:S(2)}, u32[]{:S(2)}) %collective-permute-start.11) | collective-permute-done | bytes 544 | tf_op jit(solution)/shard_map/ppermute | solution.py:20
  130.2 3.2 collective-permute-start.18
  150.8 4.3 %collective-permute-start.19 = (bf16[64,1,1,128]{3,0,1,2:T(8,128)(2,1)S(1)}, bf16[64,1,1,128]{3,0,1,2:T(8,128)(2,1)S(1)}, u32[]{:S(2)}, u32[]{:S(2)}) collective-permute-start(bf16[64,1,1,128]{3,0,1,2:T(8,128)(2,1)S(1)} %get-tuple-element.99), channel_id=1, source_target_pairs={{0,8},{8,16},{16,24},{1,9},{9,17},{17,25},{2,10},{10,18},{18,26},{... | collective-permute-start | bytes 49160 | tf_op jit(solution)/shard_map/ppermute | solution.py:18
  157.2 5.2 %all-to-all-start = ((bf16[8,2,3,4,2,128]{5,1,4,3,2,0:T(2,128)(2,1)}), bf16[8,2,3,4,2,128]{5,1,4,3,2,0:T(2,128)(2,1)S(1)}, u32[]{:S(2)}, u32[]{:S(2)}) async-start(bf16[8,2,3,4,2,128]{5,1,4,3,2,0:T(2,128)(2,1)} %broadcast_multiply_fusion), calls=%async_computation | async-start | bytes 196608 | tf_op jit(solution)/shard_map/all_to_all | solution.py:169
  163.9 3.0 collective-permute-start.21
  178.1 4.6 %collective-permute-start.23 = (bf16[32,1,2,256]{3,0,2,1:T(8,128)(2,1)S(1)}, bf16[32,1,2,256]{3,0,2,1:T(8,128)(2,1)S(1)}, u32[]{:S(2)}, u32[]{:S(2)}) collective-permute-start(bf16[32,1,2,256]{3,0,2,1:T(8,128)(2,1)S(1)} %get-tuple-element.81), channel_id=1, source_target_pairs={{0,8},{8,16},{16,24},{1,9},{9,17},{17,25},{2,10},{10,18},{18,26},{... | collective-permute-start | bytes 98312 | tf_op jit(solution)/shard_map/ppermute | solution.py:18
  185.7 2.8 collective-permute-done.24
  188.6 2.6 collective-permute-start.25
  193.0 4.8 %collective-permute-done.26 = bf16[32,6,2,1]{3,0,2,1:T(8,128)(2,1)S(1)} collective-permute-done((bf16[32,6,2,1]{3,0,2,1:T(8,128)(2,1)S(1)}, bf16[32,6,2,1]{3,0,2,1:T(8,128)(2,1)S(1)}, u32[]{:S(2)}, u32[]{:S(2)}) %collective-permute-start.26) | collective-permute-done | bytes 800 | tf_op jit(solution)/shard_map/ppermute | solution.py:20
  208.0 46.2 %all-reduce.4 = (f32[27,32]{1,0:T(8,128)}, f32[3,32]{1,0:T(4,128)}) all-reduce(f32[27,32]{1,0:T(8,128)S(1)} %bitcast.2099, f32[3,32]{1,0:T(4,128)S(1)} %copy-done.100), channel_id=1, replica_groups=mesh['gz'=4,'xy'=8] {'gz','xy'}, use_global_device_ids=true, to_apply=%region_1.2 | all-reduce | flops 960 | bytes 7680 | tf_op jit(solution)/shard_map/psum | solution.py:221
  255.1 70.5 %all-reduce.8.cloned.1.call-done = (f32[27,32,32]{2,1,0:T(8,128)}, f32[8,64,32]{1,2,0:T(8,128)}, f32[27,64,64]{2,1,0:T(8,128)}, f32[8,32,64]{2,1,0:T(8,128)}) async-done(((f32[27,32,32]{2,1,0:T(8,128)}, f32[8,64,32]{1,2,0:T(8,128)}, f32[27,64,64]{2,1,0:T(8,128)}, f32[8,32,64]{2,1,0:T(8,128)}), (f32[27,32,32]{2,1,0:T(8,128)}, f32[8,64,32]{1,2,0:T(8,128)}, f32[27,64,64]{2,1,0:T(8,128)}, ...) | async-done | bytes 684048 | tf_op jit(solution)/shard_map/psum | solution.py:221
  325.6 1.9 copy.840
  (583 shorter events, 99.0 us)
Async XLA Ops:
  7.2 126.3 %copy-start = (bf16[3,32]{1,0:T(4,128)(2,1)S(1)}, bf16[3,32]{1,0:T(4,128)(2,1)}, u32[]{:S(2)}) copy-start(bf16[3,32]{1,0:T(4,128)(2,1)} %param.19) | copy-start | bytes 580
  7.2 65.9 %collective-permute-start.12 = (bf16[1,1,4,3,4,2,128]{6,5,4,3,2,1,0:T(2,128)(2,1)}, bf16[1,1,4,3,4,2,128]{6,5,4,3,2,1,0:T(2,128)(2,1)S(1)}, u32[]{:S(2)}, u32[]{:S(2)}) collective-permute-start(bf16[1,1,4,3,4,2,128]{6,5,4,3,2,1,0:T(2,128)(2,1)} %param.11), channel_id=1, source_target_pairs={{0,1},{1,2},{2,3},{3,4},{4,5},{5,6},{6,7},{7,0},{8,9},{9,10},{10,1... | collective-permute-start | bytes 73736 | tf_op jit(solution)/shard_map/ppermute | solution.py:106
  7.7 65.4 %collective-permute-start.13 = (bf16[1,1,4,3,4,2,128]{6,5,4,3,2,1,0:T(2,128)(2,1)}, bf16[1,1,4,3,4,2,128]{6,5,4,3,2,1,0:T(2,128)(2,1)S(1)}, u32[]{:S(2)}, u32[]{:S(2)}) collective-permute-start(bf16[1,1,4,3,4,2,128]{6,5,4,3,2,1,0:T(2,128)(2,1)} %param.11), channel_id=1, source_target_pairs={{0,7},{1,0},{2,1},{3,2},{4,3},{5,4},{6,5},{7,6},{8,15},{9,8},{10,9... | collective-permute-start | bytes 73736 | tf_op jit(solution)/shard_map/ppermute | solution.py:111
  39.5 18.8 %collective-permute-start = (bf16[1,1,2,256]{3,2,1,0:T(2,128)(2,1)S(1)}, bf16[1,1,2,256]{3,2,1,0:T(2,128)(2,1)S(1)}, u32[]{:S(2)}, u32[]{:S(2)}) collective-permute-start(bf16[1,1,2,256]{3,2,1,0:T(2,128)(2,1)S(1)} %get-tuple-element.194), channel_id=1, source_target_pairs={{0,8},{8,16},{16,24},{1,9},{9,17},{17,25},{2,10},{10,18},{18,26},{... | collective-permute-start | bytes 3080 | tf_op jit(solution)/shard_map/ppermute | solution.py:18
  43.0 15.3 %collective-permute-start.1 = (bf16[1,1,2,256]{3,2,1,0:T(2,128)(2,1)S(1)}, bf16[1,1,2,256]{3,2,1,0:T(2,128)(2,1)S(1)}, u32[]{:S(2)}, u32[]{:S(2)}) collective-permute-start(bf16[1,1,2,256]{3,2,1,0:T(2,128)(2,1)S(1)} %get-tuple-element.193), channel_id=1, source_target_pairs={{8,0},{16,8},{24,16},{9,1},{17,9},{25,17},{10,2},{18,10},{26,18},{... | collective-permute-start | bytes 3080 | tf_op jit(solution)/shard_map/ppermute | solution.py:20
  59.0 3.3 collective-permute-start.2
  60.9 3.8 %collective-permute-start.3 = (bf16[1,6,2,1]{3,2,1,0:T(2,128)(2,1)S(1)}, bf16[1,6,2,1]{3,2,1,0:T(2,128)(2,1)S(1)}, u32[]{:S(2)}, u32[]{:S(2)}) collective-permute-start(bf16[1,6,2,1]{3,2,1,0:T(2,128)(2,1)S(1)} %get-tuple-element.185), channel_id=1, source_target_pairs={{1,0},{2,1},{3,2},{4,3},{5,4},{6,5},{7,6},{9,8},{10,9},{11,10},{12... | collective-permute-start | bytes 80 | tf_op jit(solution)/shard_map/ppermute | solution.py:20
  67.1 12.4 %collective-permute-start.4 = (bf16[32,1,2,256]{3,0,2,1:T(8,128)(2,1)S(1)}, bf16[32,1,2,256]{3,0,2,1:T(8,128)(2,1)S(1)}, u32[]{:S(2)}, u32[]{:S(2)}) collective-permute-start(bf16[32,1,2,256]{3,0,2,1:T(8,128)(2,1)S(1)} %get-tuple-element.91), channel_id=1, source_target_pairs={{0,8},{8,16},{16,24},{1,9},{9,17},{17,25},{2,10},{10,18},{18,26},{... | collective-permute-start | bytes 98312 | tf_op jit(solution)/shard_map/ppermute | solution.py:18
  71.6 7.9 %collective-permute-start.5 = (bf16[32,1,2,256]{3,0,2,1:T(8,128)(2,1)S(1)}, bf16[32,1,2,256]{3,0,2,1:T(8,128)(2,1)S(1)}, u32[]{:S(2)}, u32[]{:S(2)}) collective-permute-start(bf16[32,1,2,256]{3,0,2,1:T(8,128)(2,1)S(1)} %get-tuple-element.92), channel_id=1, source_target_pairs={{8,0},{16,8},{24,16},{9,1},{17,9},{25,17},{10,2},{18,10},{26,18},{... | collective-permute-start | bytes 98312 | tf_op jit(solution)/shard_map/ppermute | solution.py:20
  76.8 31.5 %collective-permute-start.14 = (bf16[1,1,4,3,4,2,128]{6,5,4,3,2,1,0:T(2,128)(2,1)S(1)}, bf16[1,1,4,3,4,2,128]{6,5,4,3,2,1,0:T(2,128)(2,1)}, u32[]{:S(2)}, u32[]{:S(2)}) collective-permute-start(bf16[1,1,4,3,4,2,128]{6,5,4,3,2,1,0:T(2,128)(2,1)S(1)} %collective-permute-done.12), channel_id=1, source_target_pairs={{0,1},{1,2},{2,3},{3,4},{4,5},{5,6},{6,7},{7,0},{8,9},{9,10},{10,1... | collective-permute-start | bytes 73736 | tf_op jit(solution)/shard_map/ppermute | solution.py:106
  78.9 30.2 %collective-permute-start.15 = (bf16[1,1,4,3,4,2,128]{6,5,4,3,2,1,0:T(2,128)(2,1)S(1)}, bf16[1,1,4,3,4,2,128]{6,5,4,3,2,1,0:T(2,128)(2,1)}, u32[]{:S(2)}, u32[]{:S(2)}) collective-permute-start(bf16[1,1,4,3,4,2,128]{6,5,4,3,2,1,0:T(2,128)(2,1)S(1)} %collective-permute-done.13), channel_id=1, source_target_pairs={{0,7},{1,0},{2,1},{3,2},{4,3},{5,4},{6,5},{7,6},{8,15},{9,8},{10,9... | collective-permute-start | bytes 73736 | tf_op jit(solution)/shard_map/ppermute | solution.py:111
  79.6 3.6 %collective-permute-start.6 = (bf16[32,6,2,1]{3,0,2,1:T(8,128)(2,1)S(1)}, bf16[32,6,2,1]{3,0,2,1:T(8,128)(2,1)S(1)}, u32[]{:S(2)}, u32[]{:S(2)}) collective-permute-start(bf16[32,6,2,1]{3,0,2,1:T(8,128)(2,1)S(1)} %get-tuple-element.79), channel_id=1, source_target_pairs={{0,1},{1,2},{2,3},{3,4},{4,5},{5,6},{6,7},{8,9},{9,10},{10,11},{11... | collective-permute-start | bytes 2312 | tf_op jit(solution)/shard_map/ppermute | solution.py:18
  81.5 4.7 %collective-permute-start.7 = (bf16[32,6,2,1]{3,0,2,1:T(8,128)(2,1)S(1)}, bf16[32,6,2,1]{3,0,2,1:T(8,128)(2,1)S(1)}, u32[]{:S(2)}, u32[]{:S(2)}) collective-permute-start(bf16[32,6,2,1]{3,0,2,1:T(8,128)(2,1)S(1)} %get-tuple-element.80), channel_id=1, source_target_pairs={{1,0},{2,1},{3,2},{4,3},{5,4},{6,5},{7,6},{9,8},{10,9},{11,10},{12... | collective-permute-start | bytes 2312 | tf_op jit(solution)/shard_map/ppermute | solution.py:20
  102.6 13.9 %collective-permute-start.8 = (bf16[64,1,1,128]{3,0,1,2:T(8,128)(2,1)S(1)}, bf16[64,1,1,128]{3,0,1,2:T(8,128)(2,1)S(1)}, u32[]{:S(2)}, u32[]{:S(2)}) collective-permute-start(bf16[64,1,1,128]{3,0,1,2:T(8,128)(2,1)S(1)} %get-tuple-element.101), channel_id=1, source_target_pairs={{0,8},{8,16},{16,24},{1,9},{9,17},{17,25},{2,10},{10,18},{18,26},{... | collective-permute-start | bytes 49160 | tf_op jit(solution)/shard_map/ppermute | solution.py:18
  106.9 9.6 %collective-permute-start.9 = (bf16[64,1,1,128]{3,0,1,2:T(8,128)(2,1)S(1)}, bf16[64,1,1,128]{3,0,1,2:T(8,128)(2,1)S(1)}, u32[]{:S(2)}, u32[]{:S(2)}) collective-permute-start(bf16[64,1,1,128]{3,0,1,2:T(8,128)(2,1)S(1)} %get-tuple-element.102), channel_id=1, source_target_pairs={{8,0},{16,8},{24,16},{9,1},{17,9},{25,17},{10,2},{18,10},{26,18},{... | collective-permute-start | bytes 49160 | tf_op jit(solution)/shard_map/ppermute | solution.py:20
  113.4 16.8 %collective-permute-start.16 = (bf16[1,1,4,3,4,2,128]{6,5,4,3,2,1,0:T(2,128)(2,1)}, bf16[1,1,4,3,4,2,128]{6,5,4,3,2,1,0:T(2,128)(2,1)S(1)}, u32[]{:S(2)}, u32[]{:S(2)}) collective-permute-start(bf16[1,1,4,3,4,2,128]{6,5,4,3,2,1,0:T(2,128)(2,1)} %collective-permute-done.14), channel_id=1, source_target_pairs={{0,1},{1,2},{2,3},{3,4},{4,5},{5,6},{6,7},{7,0},{8,9},{9,10},{10,1... | collective-permute-start | bytes 73736 | tf_op jit(solution)/shard_map/ppermute | solution.py:106
  116.4 17.2 %collective-permute-start.17 = (bf16[1,1,4,3,4,2,128]{6,5,4,3,2,1,0:T(2,128)(2,1)}, bf16[1,1,4,3,4,2,128]{6,5,4,3,2,1,0:T(2,128)(2,1)S(1)}, u32[]{:S(2)}, u32[]{:S(2)}) collective-permute-start(bf16[1,1,4,3,4,2,128]{6,5,4,3,2,1,0:T(2,128)(2,1)} %collective-permute-done.15), channel_id=1, source_target_pairs={{0,7},{1,0},{2,1},{3,2},{4,3},{5,4},{6,5},{7,6},{8,15},{9,8},{10,9... | collective-permute-start | bytes 73736 | tf_op jit(solution)/shard_map/ppermute | solution.py:111
  116.6 9.1 %collective-permute-start.10 = (bf16[64,4,1,1]{3,0,1,2:T(8,128)(2,1)S(1)}, bf16[64,4,1,1]{3,0,1,2:T(8,128)(2,1)S(1)}, u32[]{:S(2)}, u32[]{:S(2)}) collective-permute-start(bf16[64,4,1,1]{3,0,1,2:T(8,128)(2,1)S(1)} %get-tuple-element.95), channel_id=1, source_target_pairs={{0,1},{1,2},{2,3},{3,4},{4,5},{5,6},{6,7},{8,9},{9,10},{10,11},{11... | collective-permute-start | bytes 1544 | tf_op jit(solution)/shard_map/ppermute | solution.py:18
  119.1 6.3 %collective-permute-start.11 = (bf16[64,4,1,1]{3,0,1,2:T(8,128)(2,1)S(1)}, bf16[64,4,1,1]{3,0,1,2:T(8,128)(2,1)S(1)}, u32[]{:S(2)}, u32[]{:S(2)}) collective-permute-start(bf16[64,4,1,1]{3,0,1,2:T(8,128)(2,1)S(1)} %get-tuple-element.96), channel_id=1, source_target_pairs={{1,0},{2,1},{3,2},{4,3},{5,4},{6,5},{7,6},{9,8},{10,9},{11,10},{12... | collective-permute-start | bytes 1544 | tf_op jit(solution)/shard_map/ppermute | solution.py:20
  130.2 7.0 %collective-permute-start.18 = (bf16[1,1,4,3,4,2,128]{6,5,4,3,2,1,0:T(2,128)(2,1)S(1)}, bf16[1,1,4,3,4,2,128]{6,5,4,3,2,1,0:T(2,128)(2,1)S(1)}, u32[]{:S(2)}, u32[]{:S(2)}) collective-permute-start(bf16[1,1,4,3,4,2,128]{6,5,4,3,2,1,0:T(2,128)(2,1)S(1)} %collective-permute-done.16), channel_id=1, source_target_pairs={{0,1},{1,2},{2,3},{3,4},{4,5},{5,6},{6,7},{7,0},{8,9},{9,10},{10,1... | collective-permute-start | bytes 73736 | tf_op jit(solution)/shard_map/ppermute | solution.py:106
  150.8 11.7 %collective-permute-start.19 = (bf16[64,1,1,128]{3,0,1,2:T(8,128)(2,1)S(1)}, bf16[64,1,1,128]{3,0,1,2:T(8,128)(2,1)S(1)}, u32[]{:S(2)}, u32[]{:S(2)}) collective-permute-start(bf16[64,1,1,128]{3,0,1,2:T(8,128)(2,1)S(1)} %get-tuple-element.99), channel_id=1, source_target_pairs={{0,8},{8,16},{16,24},{1,9},{9,17},{17,25},{2,10},{10,18},{18,26},{... | collective-permute-start | bytes 49160 | tf_op jit(solution)/shard_map/ppermute | solution.py:18
  155.1 7.4 %collective-permute-start.20 = (bf16[64,1,1,128]{3,0,1,2:T(8,128)(2,1)S(1)}, bf16[64,1,1,128]{3,0,1,2:T(8,128)(2,1)S(1)}, u32[]{:S(2)}, u32[]{:S(2)}) collective-permute-start(bf16[64,1,1,128]{3,0,1,2:T(8,128)(2,1)S(1)} %get-tuple-element.100), channel_id=1, source_target_pairs={{8,0},{16,8},{24,16},{9,1},{17,9},{25,17},{10,2},{18,10},{26,18},{... | collective-permute-start | bytes 49160 | tf_op jit(solution)/shard_map/ppermute | solution.py:20
  157.2 96.9 %all-to-all-start = ((bf16[8,2,3,4,2,128]{5,1,4,3,2,0:T(2,128)(2,1)}), bf16[8,2,3,4,2,128]{5,1,4,3,2,0:T(2,128)(2,1)S(1)}, u32[]{:S(2)}, u32[]{:S(2)}) async-start(bf16[8,2,3,4,2,128]{5,1,4,3,2,0:T(2,128)(2,1)} %broadcast_multiply_fusion), calls=%async_computation | async-start | bytes 196608 | tf_op jit(solution)/shard_map/all_to_all | solution.py:169
  162.4 163.1 %all-reduce.8.cloned.1.call-start = ((), (), s32[]{:S(2)}) async-start(), calls=%async_computation.1 | async-start | bytes 3178496 | tf_op jit(solution)/shard_map/psum | solution.py:221
  162.6 4.5 %collective-permute-start.22 = (bf16[64,4,1,1]{3,0,1,2:T(8,128)(2,1)S(1)}, bf16[64,4,1,1]{3,0,1,2:T(8,128)(2,1)S(1)}, u32[]{:S(2)}, u32[]{:S(2)}) collective-permute-start(bf16[64,4,1,1]{3,0,1,2:T(8,128)(2,1)S(1)} %get-tuple-element.94), channel_id=1, source_target_pairs={{1,0},{2,1},{3,2},{4,3},{5,4},{6,5},{7,6},{9,8},{10,9},{11,10},{12... | collective-permute-start | bytes 1544 | tf_op jit(solution)/shard_map/ppermute | solution.py:20
  163.9 3.9 %collective-permute-start.21 = (bf16[64,4,1,1]{3,0,1,2:T(8,128)(2,1)S(1)}, bf16[64,4,1,1]{3,0,1,2:T(8,128)(2,1)S(1)}, u32[]{:S(2)}, u32[]{:S(2)}) collective-permute-start(bf16[64,4,1,1]{3,0,1,2:T(8,128)(2,1)S(1)} %get-tuple-element.93), channel_id=1, source_target_pairs={{0,1},{1,2},{2,3},{3,4},{4,5},{5,6},{6,7},{8,9},{9,10},{10,11},{11... | collective-permute-start | bytes 1544 | tf_op jit(solution)/shard_map/ppermute | solution.py:18
  178.1 7.6 %collective-permute-start.23 = (bf16[32,1,2,256]{3,0,2,1:T(8,128)(2,1)S(1)}, bf16[32,1,2,256]{3,0,2,1:T(8,128)(2,1)S(1)}, u32[]{:S(2)}, u32[]{:S(2)}) collective-permute-start(bf16[32,1,2,256]{3,0,2,1:T(8,128)(2,1)S(1)} %get-tuple-element.81), channel_id=1, source_target_pairs={{0,8},{8,16},{16,24},{1,9},{9,17},{17,25},{2,10},{10,18},{18,26},{... | collective-permute-start | bytes 98312 | tf_op jit(solution)/shard_map/ppermute | solution.py:18
  182.7 5.8 %collective-permute-start.24 = (bf16[32,1,2,256]{3,0,2,1:T(8,128)(2,1)S(1)}, bf16[32,1,2,256]{3,0,2,1:T(8,128)(2,1)S(1)}, u32[]{:S(2)}, u32[]{:S(2)}) collective-permute-start(bf16[32,1,2,256]{3,0,2,1:T(8,128)(2,1)S(1)} %get-tuple-element.82), channel_id=1, source_target_pairs={{8,0},{16,8},{24,16},{9,1},{17,9},{25,17},{10,2},{18,10},{26,18},{... | collective-permute-start | bytes 98312 | tf_op jit(solution)/shard_map/ppermute | solution.py:20
  188.6 4.3 %collective-permute-start.25 = (bf16[32,6,2,1]{3,0,2,1:T(8,128)(2,1)S(1)}, bf16[32,6,2,1]{3,0,2,1:T(8,128)(2,1)S(1)}, u32[]{:S(2)}, u32[]{:S(2)}) collective-permute-start(bf16[32,6,2,1]{3,0,2,1:T(8,128)(2,1)S(1)} %get-tuple-element.75), channel_id=1, source_target_pairs={{0,1},{1,2},{2,3},{3,4},{4,5},{5,6},{6,7},{8,9},{9,10},{10,11},{11... | collective-permute-start | bytes 2312 | tf_op jit(solution)/shard_map/ppermute | solution.py:18
  191.2 6.5 %collective-permute-start.26 = (bf16[32,6,2,1]{3,0,2,1:T(8,128)(2,1)S(1)}, bf16[32,6,2,1]{3,0,2,1:T(8,128)(2,1)S(1)}, u32[]{:S(2)}, u32[]{:S(2)}) collective-permute-start(bf16[32,6,2,1]{3,0,2,1:T(8,128)(2,1)S(1)} %get-tuple-element.76), channel_id=1, source_target_pairs={{1,0},{2,1},{3,2},{4,3},{5,4},{6,5},{7,6},{9,8},{10,9},{11,10},{12... | collective-permute-start | bytes 2312 | tf_op jit(solution)/shard_map/ppermute | solution.py:20
  206.5 47.7 %copy-start.101 = (s32[1,1,4]{2,1,0:T(1,128)S(1)}, s32[1,1,4]{2,1,0:T(1,128)}, u32[]{:S(2)}) copy-start(s32[1,1,4]{2,1,0:T(1,128)} %param.13) | copy-start | bytes 52
  206.5 47.7 %copy-start.102 = (pred[4]{0:T(512)(128)(4,1)S(1)}, pred[4]{0:T(512)(128)(4,1)}, u32[]{:S(2)}) copy-start(pred[4]{0:T(512)(128)(4,1)} %iota_compare_fusion.8) | copy-start | bytes 16
  (100 other events, 422.5 us)
Sparse Core Ops, SparseCore 0:
  185.8 139.7 all-reduce.7
